TPU v7x, 256 devices: a whole 4x4x8 slice. The times are simulated.
256 devices in a mesh: blk: 32 (over x, y, core), row: 8 (over z).
Axes of the slice: x: 4, y: 4, z: 8, core: 2. Of those that a mesh axis runs over, the one named last changes fastest.
Arguments:
- samples: bfloat16 [1024, 8192], P('blk', 'row'), may hold values from -8 to 8, as said below
- blocks: int32 [64, 4], replicated, may hold values from 0 to 31
- factor: float32 [64, 1024], P(None, 'row'), may hold values from -1.2 to 1.2
Outputs:
- cumulants: float32 [64, 1024, 1024], P('blk', 'row')
- factor_out: float32 [64, 1024], P(None, 'row')
Inputs may be any that keep to these rules, and one draw needn't show every extreme that they name: `samples`: channel values are drawn with mean zero.
All inputs are finite; a program needn't handle non-finite values.
Results may differ from a plain program's by a relative error of at most 0.0014.
Values may be sent and summed in bfloat16 or wider, within the bound.
No kernel may reach another device: no remote copies, remote signals or barrier semaphores. Data moves between devices by JAX's collectives and lax.ppermute only.
A program may use at most 64 MiB of HBM per device.

v0:
```python
import jax
import jax.numpy as jnp
from jax import lax
from jax.sharding import PartitionSpec as P

CHANNELS = 1024
BLOCK = 32
RANK = 64
SAMPLES = 8192
ITERS = 2
step_size = 0.2


def pair_rows(left, right):
    product = left[:, None, :].astype(jnp.float32) * right[None, :, :].astype(jnp.float32)
    return product.reshape(left.shape[0] * right.shape[0], left.shape[1]).astype(jnp.bfloat16)


def contract_last(left, right):
    return lax.dot_general(
        left, right, (((1,), (1,)), ((), ())), preferred_element_type=jnp.float32
    )


def gauss_terms(gram, count, width, row_lo):
    highest = lax.Precision.HIGHEST

    def part(first, second):
        return gram[first * width : (first + 1) * width, second * width : (second + 1) * width]

    cov_ab = lax.dynamic_slice_in_dim(part(0, 1), row_lo, count, 0)
    cov_ac = lax.dynamic_slice_in_dim(part(0, 2), row_lo, count, 0)
    cov_ad = lax.dynamic_slice_in_dim(part(0, 3), row_lo, count, 0)
    cov_cd = part(2, 3)
    cov_bd = part(1, 3)
    cov_bc = part(1, 2)
    first_term = cov_ab.reshape(-1)[:, None] * cov_cd.reshape(-1)[None, :]
    second_term = jnp.einsum("ik,jl->ijkl", cov_ac, cov_bd, precision=highest).reshape(
        count * width, width * width
    )
    third_term = jnp.einsum("il,jk->ijkl", cov_ad, cov_bc, precision=highest).reshape(
        count * width, width * width
    )
    return first_term + second_term + third_term


def add_cols(total, piece, start):
    old = lax.dynamic_slice_in_dim(total, start, piece.shape[1], 1)
    return lax.dynamic_update_slice_in_dim(total, old + piece, start, 1)


def add_grads(total, kslab, full, ids, row_lo, count, width):
    highest = lax.Precision.HIGHEST
    rank = full.shape[0]
    start_a = ids[0] * width + row_lo
    fac_a = lax.dynamic_slice_in_dim(full, start_a, count, 1)
    fac_b = lax.dynamic_slice_in_dim(full, ids[1] * width, width, 1)
    fac_c = lax.dynamic_slice_in_dim(full, ids[2] * width, width, 1)
    fac_d = lax.dynamic_slice_in_dim(full, ids[3] * width, width, 1)
    upair = (fac_a[:, :, None] * fac_b[:, None, :]).reshape(rank, count * width)
    vpair = (fac_c[:, :, None] * fac_d[:, None, :]).reshape(rank, width * width)
    model = lax.dot_general(upair, vpair, (((0,), (0,)), ((), ())), precision=highest)
    resid = kslab - model
    wmat = lax.dot_general(vpair, resid, (((1,), (1,)), ((), ())), precision=highest).reshape(
        rank, count, width
    )
    zmat = jnp.dot(upair, resid, precision=highest).reshape(rank, width, width)
    total = add_cols(total, jnp.sum(wmat * fac_b[:, None, :], axis=2), start_a)
    total = add_cols(total, jnp.sum(wmat * fac_a[:, :, None], axis=1), ids[1] * width)
    total = add_cols(total, jnp.sum(zmat * fac_d[:, None, :], axis=2), ids[2] * width)
    total = add_cols(total, jnp.sum(zmat * fac_c[:, :, None], axis=1), ids[3] * width)
    return total


def gather_factor(columns):
    return lax.all_gather(columns, "row", axis=1, tiled=True)


def per_device(samples, blocks, factor):
    width = BLOCK
    row_count = lax.axis_size("row")
    count = width // row_count
    row_lo = lax.axis_index("row") * count
    per_owner = blocks.shape[0] // lax.axis_size("blk")
    mine = lax.dynamic_slice_in_dim(blocks, lax.axis_index("blk") * per_owner, per_owner, 0)
    needed = mine.reshape(-1)
    pairs = width * width
    piece = lax.all_gather(samples, "blk", axis=0, tiled=True)
    pieces = piece.shape[0] // width
    owned = jnp.arange(pieces, dtype=jnp.int32)
    select = (needed[:, None] == owned[None, :]).astype(jnp.bfloat16)
    shaped = piece.reshape(pieces, width, piece.shape[1])
    taken = jnp.einsum("mb,bcs->mcs", select, shaped, preferred_element_type=jnp.float32)
    local = taken.astype(jnp.bfloat16)
    slabs = []
    whole = lax.all_gather(local, "row", axis=2, tiled=True)
    sample_block = min(SAMPLES, 2048)
    for slot in range(per_owner):
        source_a = whole[4 * slot]
        source_b = whole[4 * slot + 1]
        source_c = whole[4 * slot + 2]
        source_d = whole[4 * slot + 3]

        def accumulate(index, moment):
            low = index * sample_block
            left = lax.dynamic_slice(source_a, (row_lo, low), (count, sample_block))
            right = lax.dynamic_slice_in_dim(source_b, low, sample_block, 1)
            third = lax.dynamic_slice_in_dim(source_c, low, sample_block, 1)
            fourth = lax.dynamic_slice_in_dim(source_d, low, sample_block, 1)
            pmat = pair_rows(left, right)
            qmat = pair_rows(third, fourth)
            return moment + contract_last(pmat, qmat)

        moment = lax.fori_loop(
            0, SAMPLES // sample_block, accumulate, jnp.zeros((count * width, pairs), jnp.float32)
        )
        moment = moment / SAMPLES
        joined = whole[4 * slot : 4 * slot + 4].reshape(4 * width, whole.shape[2])
        gram = contract_last(joined, joined) / SAMPLES
        slabs.append(moment - gauss_terms(gram, count, width, row_lo))
    columns = factor
    full = gather_factor(columns)
    for step in range(ITERS):
        grad = jnp.zeros(full.shape, jnp.float32)
        for slot in range(per_owner):
            grad = add_grads(grad, slabs[slot], full, mine[slot], row_lo, count, width)
        owned_cols = lax.psum_scatter(grad, "row", scatter_dimension=1, tiled=True)
        owned_cols = lax.psum(owned_cols, "blk")
        squares = lax.psum(jnp.sum(owned_cols * owned_cols), "row")
        scale = lax.rsqrt(squares / (RANK * CHANNELS) + 1e-06)
        columns = columns + step_size * scale * owned_cols
        if step + 1 < ITERS:
            full = gather_factor(columns)
    return (jnp.stack(slabs), columns)


def solution(mesh):
    placed = (P("blk", "row"), P(), P(None, "row"))
    return jax.shard_map(
        per_device,
        mesh=mesh,
        in_specs=placed,
        out_specs=(P("blk", "row", None), P(None, "row")),
        check_vma=False,
    )
```

profile of v0, /device:TPU:32, one launch (start us, length us, event | category | flops | bytes accessed | tf_op | source)
XLA Modules:
  0.0 646.9 jit_solution(17991353607669108797)
XLA Ops:
  8.2 53.5 %all-gather.3.cloned.1.call-done = bf16[1024,1024]{1,0:T(8,128)(2,1)} async-done(((bf16[32,1024]{1,0:T(8,128)(2,1)}), bf16[1024,1024]{1,0:T(8,128)(2,1)}) %all-gather.3.cloned.1.call-update) | async-done | bytes 2097168 | tf_op jit(solution)/shard_map/all_gather | solution.py:88
  61.8 4.7 fusion.2
  72.3 26.5 %all_gather.14 = f32[64,1024]{1,0:T(8,128)S(1)} all-gather(f32[64,128]{1,0:T(8,128)S(1)} %copy-done.11), channel_id=1, replica_groups=mesh['blk'=32,'row'=8] {'row'}, dimensions={1}, use_global_device_ids=true | all-gather | bytes 294912 | tf_op jit(solution)/shard_map/all_gather | solution.py:76
  101.3 19.8 %all-gather.5.cloned.1.call-done = bf16[8,32,8192]{2,0,1:T(8,128)(2,1)} async-done(((bf16[8,32,1024]{2,0,1:T(8,128)(2,1)}), bf16[8,32,8192]{2,0,1:T(8,128)(2,1)}) %all-gather.5.cloned.1.call-update) | async-done | bytes 4194320 | tf_op jit(solution)/shard_map/all_gather | solution.py:96
  121.1 21.7 %fusion.10 = (bf16[1,32,8192]{2,0,1:T(2,128)(2,1)S(1)}, bf16[1,32,8192]{2,0,1:T(2,128)(2,1)}, bf16[1,32,8192]{2,0,1:T(2,128)(2,1)}, bf16[1,32,8192]{2,0,1:T(2,12...) fusion(bf16[8,32,8192]{2,0,1:T(8,128)(2,1)} %all-gather.5.clone, ...), kind=kLoop, calls=%fused_computation.112 | loop fusion | bytes 8388608 | tf_op jit(solution)/shard_map/slice | solution.py:102
  145.9 31.4 %while.32 = (s32[]{:T(128)}, f32[128,1024]{1,0:T(8,128)S(1)}, bf16[32,8192]{1,0:T(8,128)(2,1)}, s32[]{:T(128)}, bf16[32,8192]{1,0:T(8,128)(2,1)S(1)}, /*index=5*...) while((s32[]{:T(128)}, f32[128,1024]{1,0:T(8,128)S(1)}, ...), condition=%wide.region_1.0_spmd.clone, body=%wide.region_0.0_spmd.clone.sunk | while | flops 542056448 | bytes 12533941 | solution.py:114
  150.0 3.8 convolution_add_fusion.4
  157.9 3.8 convolution_add_fusion.4
  165.7 3.8 convolution_add_fusion.4
  173.6 3.8 convolution_add_fusion.4
  177.4 6.7 %fusion.11 = (bf16[4,32,8192]{2,0,1:T(4,128)(2,1)S(1)}, bf16[4,32,8192]{2,0,1:T(4,128)(2,1)}) fusion(bf16[8,32,8192]{2,0,1:T(8,128)(2,1)} %all-gather.5.cloned.1.call-done), kind=kLoop, calls=%fused_computation.113 | loop fusion | bytes 8388608 | tf_op jit(solution)/shard_map/slice | solution.py:118
  197.6 3.6 copy_bitcast_fusion.2
  203.3 35.3 %while.33 = (s32[]{:T(128)}, f32[128,1024]{1,0:T(8,128)S(1)}, bf16[32,8192]{1,0:T(8,128)(2,1)}, s32[]{:T(128)}, bf16[32,8192]{1,0:T(8,128)(2,1)S(1)}, /*index=5*...) while((s32[]{:T(128)}, f32[128,1024]{1,0:T(8,128)S(1)}, ...), condition=%wide.region_3.0_spmd.clone, body=%wide.region_2.0_spmd.clone.sunk | while | flops 542056448 | bytes 12533941 | solution.py:114
  208.2 3.8 convolution_add_fusion.5
  217.0 3.8 convolution_add_fusion.5
  225.8 3.8 convolution_add_fusion.5
  234.6 3.8 convolution_add_fusion.5
  250.8 37.1 %reduce-scatter.3.cloned.1.call-done = f32[64,128]{0,1:T(8,128)} async-done(((f32[64,1024]{0,1:T(8,128)}), f32[64,128]{0,1:T(8,128)}) %reduce-scatter.3.cloned.1.call-update) | async-done | bytes 32784 | tf_op jit(solution)/shard_map/reduce_scatter | solution.py:127
  287.9 124.3 %psum.28 = f32[64,128]{0,1:T(8,128)S(1)} all-reduce(f32[64,128]{0,1:T(8,128)} %reduce-scatter.3.cloned.1.call-done), channel_id=1, replica_groups=mesh['blk'=32,'row'=8] {'blk'}, use_global_device_ids=true, to_apply=%region_13.0 | all-reduce | flops 8192 | bytes 65536 | tf_op jit(solution)/shard_map/psum | solution.py:128
  412.9 16.0 %psum.29 = f32[]{:T(128)} all-reduce(f32[]{:T(128)} %multiply_reduce_fusion.13), channel_id=1, replica_groups=mesh['blk'=32,'row'=8] {'row'}, use_global_device_ids=true, to_apply=%region_15.0 | all-reduce | flops 1 | bytes 8 | tf_op jit(solution)/shard_map/psum | solution.py:129
  429.7 24.3 %all_gather.15 = f32[64,1024]{0,1:T(8,128)S(1)} all-gather(f32[64,128]{0,1:T(8,128)S(1)} %multiply_add_fusion.1), channel_id=1, replica_groups=mesh['blk'=32,'row'=8] {'row'}, dimensions={1}, use_global_device_ids=true | all-gather | bytes 294912 | tf_op jit(solution)/shard_map/all_gather | solution.py:76
  463.1 34.0 %reduce-scatter.5.cloned.1.call-done = f32[64,128]{0,1:T(8,128)} async-done(((f32[64,1024]{0,1:T(8,128)}), f32[64,128]{0,1:T(8,128)}) %reduce-scatter.5.cloned.1.call-update) | async-done | bytes 32784 | tf_op jit(solution)/shard_map/reduce_scatter | solution.py:127
  497.1 124.3 %psum.30 = f32[64,128]{0,1:T(8,128)S(1)} all-reduce(f32[64,128]{0,1:T(8,128)} %reduce-scatter.5.cloned.1.call-done), channel_id=1, replica_groups=mesh['blk'=32,'row'=8] {'blk'}, use_global_device_ids=true, to_apply=%region_25.0 | all-reduce | flops 8192 | bytes 65536 | tf_op jit(solution)/shard_map/psum | solution.py:128
  623.1 15.9 %psum.31 = f32[]{:T(128)} all-reduce(f32[]{:T(128)} %multiply_reduce_fusion.8), channel_id=1, replica_groups=mesh['blk'=32,'row'=8] {'row'}, use_global_device_ids=true, to_apply=%region_27.0 | all-reduce | flops 1 | bytes 8 | tf_op jit(solution)/shard_map/psum | solution.py:129
  (167 shorter events, 82.9 us)
Async XLA Ops:
  7.2 0.8 copy-start
  7.2 65.1 %copy-start.11 = (f32[64,128]{1,0:T(8,128)S(1)}, f32[64,128]{1,0:T(8,128)}, u32[]{:S(2)}) copy-start(f32[64,128]{1,0:T(8,128)} %param.9) | copy-start | bytes 98308
  7.2 54.6 %all-gather.3.cloned.1.call-start = ((), (), s32[]{:S(2)}) async-start(), calls=%async_computation.2 | async-start | bytes 2162688 | tf_op jit(solution)/shard_map/all_gather | solution.py:88
  7.9 113.2 %all-gather.5.cloned.1.call-start = ((), (), s32[]{:S(2)}) async-start(), calls=%async_computation.3 | async-start | bytes 4718592 | tf_op jit(solution)/shard_map/all_gather | solution.py:96
  66.5 221.4 %reduce-scatter.3.cloned.1.call-start = ((), (), s32[]{:S(2)}) async-start(), calls=%async_computation.4 | async-start | bytes 589824 | tf_op jit(solution)/shard_map/reduce_scatter | solution.py:127
  192.3 2.1 copy-start.12
  194.4 1.5 copy-start.2
  196.5 4.6 copy-start.4
  196.5 4.6 copy-start.6
  197.6 3.6 copy-start.7
  242.8 1.5 copy-start.1
  244.3 3.4 copy-start.3
  244.3 3.4 copy-start.5
  245.9 3.3 copy-start.10
  249.9 0.8 copy-start.9
  250.7 246.3 %reduce-scatter.5.cloned.1.call-start = ((), (), s32[]{:S(2)}) async-start(), calls=%async_computation.5 | async-start | bytes 589824 | tf_op jit(solution)/shard_map/reduce_scatter | solution.py:127
  462.3 0.8 copy-start.8
Sparse Core Ops, SparseCore 0:
  10.6 51.1 all-gather.2
  66.6 54.4 all-gather.4
  250.8 36.9 reduce-scatter.2
  463.2 33.8 reduce-scatter.4
where the time goes:
time: 648 us; the launch traced here: 647 us
  blocking collectives  331 us (51%)
  waiting for transfers between devices  145 us (22%)
  local copies, waits for them, and re-layouts  57.5 us (9%)
  matrix products  47.2 us (7%)
  other arithmetic  44.2 us (7%)
  between operations  20.7 us (3%)
    psum x2, blocking collectives, per_device(): owned_cols = lax.psum(owned_cols, 'blk')  249 us
    reduce_scatter x2, waiting for transfers between devices, per_device(): owned_cols = lax.psum_scatter(grad, 'row', scatter_dimension=1, tiled=True)  71.1 us
    all_gather x1, waiting for transfers between devices, per_device(): piece = lax.all_gather(samples, 'blk', axis=0, tiled=True)  53.5 us
    all_gather x2, blocking collectives, gather_factor(): return lax.all_gather(columns, 'row', axis=1, tiled=True)  50.7 us
    psum x2, blocking collectives, per_device(): squares = lax.psum(jnp.sum(owned_cols * owned_cols), 'row')  32 us
    dot_general x10, matrix products, contract_last(): lax.dot_general(left, right, (((1,), (1,)), ((), ())), preferred_element_...  31.6 us
    convert_element_type x16, other arithmetic, pair_rows(): product.reshape(left.shape[0] * right.shape[0], left.shape[1])  24.8 us
    slice x1, local copies, waits for them, and re-layouts, per_device(): source_d = whole[4 * slot + 3]  21.7 us
  transfers between devices with their start and end apart: 4, of which 4 were waited for; matrix products, arithmetic and copies ran while one was open for 1% of the time, Pallas kernels for 0%

commit v1 on v0

--- a/solution.py
+++ b/solution.py
@@ -9,6 +9,28 @@
 SAMPLES = 8192
 ITERS = 2
 step_size = 0.2
+
+
+def joined_along(blocks, dim):
+    dims = list(blocks.shape[1:])
+    dims[dim] *= blocks.shape[0]
+    return jnp.moveaxis(blocks, 0, dim).reshape(dims)
+
+
+def collect(x, axis, dim):
+    size = lax.axis_size(axis)
+    pairs = [(i, (i + 1) % size) for i in range(size)]
+    back = [(b, a) for a, b in pairs]
+    lower, upper = ([], [])
+    for lap in range(size - 1):
+        if lap % 2 == 0:
+            lower.append(lax.ppermute(lower[-1] if lower else x, axis, pairs))
+        else:
+            upper.append(lax.ppermute(upper[-1] if upper else x, axis, back))
+    pieces = jnp.stack([*lower[::-1], x, *upper])
+    shift = lax.axis_index(axis) - len(lower)
+    pieces = pieces[(jnp.arange(size) - shift) % size]
+    return joined_along(pieces, dim)
 
 
 def pair_rows(left, right):
@@ -73,7 +95,7 @@
 
 
 def gather_factor(columns):
-    return lax.all_gather(columns, "row", axis=1, tiled=True)
+    return collect(columns, "row", 1)
 
 
 def per_device(samples, blocks, factor):

time: 648 us -> 652 us (level)
  blocking collectives: 331 us -> 281 us
  waiting for transfers between devices: 145 us -> 172 us
  starting transfers between devices: 0.16 us -> 20.3 us
    all_gather x2 -> x0, blocking collectives: 50.7 us -> none  [gather_factor(): return lax.all_gather(columns, 'row', axis=1, tiled=True)]
    ppermute x0 -> x14, waiting for transfers between devices: none -> 21.9 us  [the longest x8 15.7 us: collect(): lower.append(lax.ppermute(lower[-1] if lower else x, axis, pairs))]
    ppermute x0 -> x14, starting transfers between devices: none -> 20.1 us  [the longest x6 11.6 us: collect(): upper.append(lax.ppermute(upper[-1] if upper else x, axis, back))]
  transfers between devices with their start and end apart: 4 -> 18, of which waited for: 4 -> 15; matrix products, arithmetic and copies ran while one was open for 1% -> 1% of each run, Pallas kernels for 0% -> 0%
where the time goes in v1:
time: 652 us; the launch traced here: 645 us
  blocking collectives  281 us (43%)
  waiting for transfers between devices  172 us (26%)
  local copies, waits for them, and re-layouts  59 us (9%)
  matrix products  48.1 us (7%)
  other arithmetic  43 us (7%)
  between operations  21.1 us (3%)
  starting transfers between devices  20.3 us (3%)
    psum x2, blocking collectives, per_device(): owned_cols = lax.psum(owned_cols, 'blk')  249 us
    reduce_scatter x2, waiting for transfers between devices, per_device(): owned_cols = lax.psum_scatter(grad, 'row', scatter_dimension=1, tiled=True)  72.3 us
    all_gather x1, waiting for transfers between devices, per_device(): piece = lax.all_gather(samples, 'blk', axis=0, tiled=True)  53.5 us
    psum x2, blocking collectives, per_device(): squares = lax.psum(jnp.sum(owned_cols * owned_cols), 'row')  31.9 us
    dot_general x10, matrix products, contract_last(): lax.dot_general(left, right, (((1,), (1,)), ((), ())), preferred_element_...  31.6 us
    convert_element_type x16, other arithmetic, pair_rows(): product.reshape(left.shape[0] * right.shape[0], left.shape[1])  24.8 us
    all_gather x1, waiting for transfers between devices, per_device(): whole = lax.all_gather(local, 'row', axis=2, tiled=True)  23.5 us
    slice x1, local copies, waits for them, and re-layouts, per_device(): source_d = whole[4 * slot + 3]  21.7 us
  transfers between devices with their start and end apart: 18, of which 15 were waited for; matrix products, arithmetic and copies ran while one was open for 1% of the time, Pallas kernels for 0%

profile of v1, /device:TPU:32, one launch (start us, length us, event | category | flops | bytes accessed | tf_op | source)
XLA Modules:
  0.0 644.7 jit_solution(1119086741036612326)
XLA Ops:
  8.2 53.5 %all-gather.3.cloned.1.call-done = bf16[1024,1024]{1,0:T(8,128)(2,1)} async-done(((bf16[32,1024]{1,0:T(8,128)(2,1)}), bf16[1024,1024]{1,0:T(8,128)(2,1)}) %all-gather.3.cloned.1.call-update) | async-done | bytes 2097168 | tf_op jit(solution)/shard_map/all_gather | solution.py:110
  61.8 4.7 fusion.2
  88.8 4.6 collective-permute-done.6
  96.6 23.5 %all-gather.5.cloned.1.call-done = bf16[8,32,8192]{2,0,1:T(8,128)(2,1)} async-done(((bf16[8,32,1024]{2,0,1:T(8,128)(2,1)}), bf16[8,32,8192]{2,0,1:T(8,128)(2,1)}) %all-gather.5.cloned.1.call-update) | async-done | bytes 4194320 | tf_op jit(solution)/shard_map/all_gather | solution.py:118
  120.1 21.7 %fusion.12 = (bf16[1,32,8192]{2,0,1:T(2,128)(2,1)}, bf16[1,32,8192]{2,0,1:T(2,128)(2,1)S(1)}, bf16[1,32,8192]{2,0,1:T(2,128)(2,1)S(1)}, bf16[1,32,8192]{2,0,1:T(...) fusion(bf16[8,32,8192]{2,0,1:T(8,128)(2,1)} %all-gather.5.clone, ...), kind=kLoop, calls=%fused_computation.138 | loop fusion | bytes 8388608 | tf_op jit(solution)/shard_map/slice | solution.py:124
  144.9 31.4 %while.33 = (s32[]{:T(128)}, f32[128,1024]{1,0:T(8,128)S(1)}, bf16[32,8192]{1,0:T(8,128)(2,1)}, s32[]{:T(128)}, bf16[32,8192]{1,0:T(8,128)(2,1)S(1)}, /*index=5*...) while((s32[]{:T(128)}, f32[128,1024]{1,0:T(8,128)S(1)}, ...), condition=%wide.region_3.0_spmd.clone, body=%wide.region_2.0_spmd.clone.sunk | while | flops 542056448 | bytes 12533941 | solution.py:136
  148.9 3.8 convolution_add_fusion.5
  156.8 3.8 convolution_add_fusion.5
  164.7 3.8 convolution_add_fusion.5
  172.5 3.8 convolution_add_fusion.5
  176.3 6.8 %fusion.13 = (bf16[4,32,8192]{2,0,1:T(4,128)(2,1)}, bf16[4,32,8192]{2,0,1:T(4,128)(2,1)S(1)}) fusion(bf16[8,32,8192]{2,0,1:T(8,128)(2,1)} %all-gather.5.cloned.1.call-done), kind=kLoop, calls=%fused_computation.139 | loop fusion | bytes 8388608 | tf_op jit(solution)/shard_map/slice | solution.py:140
  195.5 3.6 copy_bitcast_fusion.6
  201.3 35.3 %while.32 = (s32[]{:T(128)}, f32[128,1024]{1,0:T(8,128)S(1)}, bf16[32,8192]{1,0:T(8,128)(2,1)}, s32[]{:T(128)}, bf16[32,8192]{1,0:T(8,128)(2,1)S(1)}, /*index=5*...) while((s32[]{:T(128)}, f32[128,1024]{1,0:T(8,128)S(1)}, ...), condition=%wide.region_1.0_spmd.clone, body=%wide.region_0.0_spmd.clone.sunk | while | flops 542056448 | bytes 12533941 | solution.py:136
  206.2 3.8 convolution_add_fusion.4
  215.0 3.8 convolution_add_fusion.4
  223.8 3.8 convolution_add_fusion.4
  232.6 3.8 convolution_add_fusion.4
  249.7 37.5 %reduce-scatter.3.cloned.1.call-done = f32[64,128]{0,1:T(8,128)} async-done(((f32[64,1024]{0,1:T(8,128)}), f32[64,128]{0,1:T(8,128)}) %reduce-scatter.3.cloned.1.call-update) | async-done | bytes 32784 | tf_op jit(solution)/shard_map/reduce_scatter | solution.py:149
  287.2 124.3 %psum.28 = f32[64,128]{0,1:T(8,128)S(1)} all-reduce(f32[64,128]{0,1:T(8,128)} %reduce-scatter.3.cloned.1.call-done), channel_id=1, replica_groups=mesh['blk'=32,'row'=8] {'blk'}, use_global_device_ids=true, to_apply=%region_13.14 | all-reduce | flops 8192 | bytes 65536 | tf_op jit(solution)/shard_map/psum | solution.py:150
  412.3 15.9 %psum.29 = f32[]{:T(128)} all-reduce(f32[]{:T(128)} %multiply_reduce_fusion.13), channel_id=1, replica_groups=mesh['blk'=32,'row'=8] {'row'}, use_global_device_ids=true, to_apply=%region_15.16 | all-reduce | flops 1 | bytes 8 | tf_op jit(solution)/shard_map/psum | solution.py:151
  429.9 3.4 collective-permute-done.7
  459.8 34.8 %reduce-scatter.5.cloned.1.call-done = f32[64,128]{0,1:T(8,128)} async-done(((f32[64,1024]{0,1:T(8,128)}), f32[64,128]{0,1:T(8,128)}) %reduce-scatter.5.cloned.1.call-update) | async-done | bytes 32784 | tf_op jit(solution)/shard_map/reduce_scatter | solution.py:149
  494.5 124.3 %psum.30 = f32[64,128]{0,1:T(8,128)S(1)} all-reduce(f32[64,128]{0,1:T(8,128)} %reduce-scatter.5.cloned.1.call-done), channel_id=1, replica_groups=mesh['blk'=32,'row'=8] {'blk'}, use_global_device_ids=true, to_apply=%region_25.26 | all-reduce | flops 8192 | bytes 65536 | tf_op jit(solution)/shard_map/psum | solution.py:150
  620.5 16.0 %psum.31 = f32[]{:T(128)} all-reduce(f32[]{:T(128)} %multiply_reduce_fusion.8), channel_id=1, replica_groups=mesh['blk'=32,'row'=8] {'row'}, use_global_device_ids=true, to_apply=%region_27.28 | all-reduce | flops 1 | bytes 8 | tf_op jit(solution)/shard_map/psum | solution.py:151
  (214 shorter events, 118.1 us)
Async XLA Ops:
  7.2 59.4 %copy-start.12 = (f32[64,128]{1,0:T(8,128)S(1)}, f32[64,128]{1,0:T(8,128)}, u32[]{:S(2)}) copy-start(f32[64,128]{1,0:T(8,128)} %param.9) | copy-start | bytes 98308
  7.2 54.6 %all-gather.3.cloned.1.call-start = ((), (), s32[]{:S(2)}) async-start(), calls=%async_computation.2 | async-start | bytes 2162688 | tf_op jit(solution)/shard_map/all_gather | solution.py:110
  7.9 112.1 %all-gather.5.cloned.1.call-start = ((), (), s32[]{:S(2)}) async-start(), calls=%async_computation.3 | async-start | bytes 4718592 | tf_op jit(solution)/shard_map/all_gather | solution.py:118
  66.5 220.7 %reduce-scatter.3.cloned.1.call-start = ((), (), s32[]{:S(2)}) async-start(), calls=%async_computation.4 | async-start | bytes 589824 | tf_op jit(solution)/shard_map/reduce_scatter | solution.py:149
  66.6 4.0 collective-permute-start
  68.2 7.8 %collective-permute-start.4 = (f32[64,128]{1,0:T(8,128)S(1)}, f32[64,128]{1,0:T(8,128)S(1)}, u32[]{:S(2)}, u32[]{:S(2)}) collective-permute-start(f32[64,128]{1,0:T(8,128)S(1)} %copy-done.12), channel_id=1, source_target_pairs={{1,0},{2,1},{3,2},{4,3},{5,4},{6,5},{7,6},{0,7},{9,8},{10,9},{11,1... | collective-permute-start | bytes 98312 | tf_op jit(solution)/shard_map/ppermute | solution.py:29
  70.6 3.9 collective-permute-start.1
  74.5 5.3 collective-permute-start.2
  76.0 10.4 %collective-permute-start.5 = (f32[64,128]{1,0:T(8,128)S(1)}, f32[64,128]{1,0:T(8,128)S(1)}, u32[]{:S(2)}, u32[]{:S(2)}) collective-permute-start(f32[64,128]{1,0:T(8,128)S(1)} %collective-permute-done.4), channel_id=1, source_target_pairs={{1,0},{2,1},{3,2},{4,3},{5,4},{6,5},{7,6},{0,7},{9,8},{10,9},{11,1... | collective-permute-start | bytes 98312 | tf_op jit(solution)/shard_map/ppermute | solution.py:29
  79.8 8.9 %collective-permute-start.3 = (f32[64,128]{1,0:T(8,128)S(1)}, f32[64,128]{1,0:T(8,128)S(1)}, u32[]{:S(2)}, u32[]{:S(2)}) collective-permute-start(f32[64,128]{1,0:T(8,128)S(1)} %collective-permute-done.2), channel_id=1, source_target_pairs={{0,1},{1,2},{2,3},{3,4},{4,5},{5,6},{6,7},{7,0},{8,9},{9,10},{10,1... | collective-permute-start | bytes 98312 | tf_op jit(solution)/shard_map/ppermute | solution.py:27
  86.4 6.9 %collective-permute-start.6 = (f32[64,128]{1,0:T(8,128)S(1)}, f32[64,128]{1,0:T(8,128)S(1)}, u32[]{:S(2)}, u32[]{:S(2)}) collective-permute-start(f32[64,128]{1,0:T(8,128)S(1)} %collective-permute-done.5), channel_id=1, source_target_pairs={{1,0},{2,1},{3,2},{4,3},{5,4},{6,5},{7,6},{0,7},{9,8},{10,9},{11,1... | collective-permute-start | bytes 98312 | tf_op jit(solution)/shard_map/ppermute | solution.py:29
  194.5 4.6 copy-start.4
  194.5 4.6 copy-start.6
  195.5 3.6 copy-start.7
  242.3 3.3 copy-start.3
  242.3 3.3 copy-start.5
  249.7 244.9 %reduce-scatter.5.cloned.1.call-start = ((), (), s32[]{:S(2)}) async-start(), calls=%async_computation.5 | async-start | bytes 589824 | tf_op jit(solution)/shard_map/reduce_scatter | solution.py:149
  428.9 4.3 collective-permute-start.7
  433.3 4.8 collective-permute-start.8
  434.2 4.3 collective-permute-start.11
  438.1 5.5 collective-permute-start.9
  438.5 5.8 collective-permute-start.12
  443.6 5.5 collective-permute-start.10
  444.3 5.7 collective-permute-start.13
  (7 other events, 7.3 us)
Sparse Core Ops, SparseCore 0:
  10.6 51.1 all-gather.2
  66.6 53.3 all-gather.4
  249.8 37.3 reduce-scatter.2
  459.9 34.5 reduce-scatter.4
